TPU v7x, 512 devices: a whole 4x8x8 slice. The times are simulated.
512 devices in a mesh: space: 64 (over z_hi, y, core), member: 8 (over z_lo, x).
Axes of the slice: x: 4, y: 8, z: 8 (z_hi: 4, z_lo: 2; z = z_hi * 2 + z_lo), core: 2. Of those that a mesh axis runs over, the one named last changes fastest.
Arguments:
- pressure: float32 [32, 10, 131072], P('member', None, 'space'), may hold values from -6 to 6
- heat: float32 [32, 10, 131072], P('member', None, 'space'), may hold values from -6 to 6
- log_cond: float32 [10, 131072], P(None, 'space'), may hold values from -1 to 1
- log_therm: float32 [10, 131072], P(None, 'space'), may hold values from -1 to 1
- frozen: float32 [10, 131072], P(None, 'space'), may hold values from 0 to 1
- frozen_flag: int32 [10, 131072], P(None, 'space'), may hold values 0 or 1
- recharge: float32 [32, 131072], P('member', 'space'), may hold values from -6 to 6
- face_cols: int32 [4, 16384], P(None, 'space'), may hold values from 0 to 2047
- face_weight: float32 [4, 16384], P(None, 'space'), may hold values from 0.05 to 0.3
- cot_pressure: float32 [32, 10, 131072], P('member', None, 'space'), may hold values from -6 to 6
- cot_heat: float32 [32, 10, 131072], P('member', None, 'space'), may hold values from -6 to 6
Outputs:
- new_pressure: float32 [32, 10, 131072], P('member', None, 'space')
- new_heat: float32 [32, 10, 131072], P('member', None, 'space')
- adj_pressure: float32 [32, 10, 131072], P('member', None, 'space')
- adj_heat: float32 [32, 10, 131072], P('member', None, 'space')
- param_grads: float32 [2, 10, 131072], P(None, None, ('space', 'member'))
All inputs are finite; a program needn't handle non-finite values. No bound on the sum of `frozen_flag` on one device may be relied on, other than what follows from the above.
Results may differ from a plain program's by a relative error of at most 0.00007.
Values sent between devices are 32-bit elements; how exact they have to be, the bound alone decides.
No kernel may reach another device: no remote copies, remote signals or barrier semaphores. Data moves between devices by JAX's collectives and lax.ppermute only.
A program may use at most 64 MiB of HBM per device.

v0:
```python
import jax
import jax.numpy as jnp
from jax import lax
from jax.sharding import PartitionSpec as P


def from_partner(value, axis, stride):
    mask = 2**stride
    pairs = [(source, source ^ mask) for source in range(lax.axis_size(axis))]
    return lax.ppermute(value, axis, pairs)


def spread(grad_iface):
    return jnp.pad(grad_iface, ((0, 0), (0, 1), (0, 0))) - jnp.pad(
        grad_iface, ((0, 0), (1, 0), (0, 0))
    )


def selector(columns, width):
    return (columns[:, None] == jnp.arange(width, dtype=jnp.int32)[None, :]).astype(jnp.float32)


def pick(values, select):
    return jnp.einsum("...c,kc->...k", values, select, precision=lax.Precision.HIGHEST)


def place(values, select):
    return jnp.einsum("...k,kc->...c", values, select, precision=lax.Precision.HIGHEST)


def body(
    pressure,
    heat,
    log_cond,
    log_therm,
    frozen,
    frozen_flag,
    recharge,
    face_cols,
    face_weight,
    cot_pressure,
    cot_heat,
):
    rounds = face_cols.shape[0]
    width = pressure.shape[2]
    blocked = frozen * frozen_flag.astype(jnp.float32)
    selects = [selector(face_cols[index], width) for index in range(rounds)]

    def advance(p_old, t_old, log_k, log_t, far_faces):
        cond = jnp.exp(log_k - 3.0 * blocked)
        therm = jnp.exp(log_t) * (1.0 + blocked)
        flow = 0.5 * (cond[:-1] + cond[1:]) * (p_old[:, 1:] - p_old[:, :-1])
        conduct = 0.5 * (therm[:-1] + therm[1:]) * (t_old[:, 1:] - t_old[:, :-1])
        carried = flow * 0.5 * (t_old[:, :-1] + t_old[:, 1:])
        p_rate = spread(flow)
        p_rate = p_rate.at[:, 0].add(recharge)
        t_rate = spread(conduct) + 0.5 * spread(carried)
        fields = jnp.stack([p_old, t_old])
        coeffs = jnp.stack([cond, therm])
        for index in range(rounds):
            select = selects[index]
            weight = face_weight[index]
            own = pick(fields, select)
            coef = pick(coeffs, select)
            update = weight * coef[:, None] * (far_faces[index] - own)
            added = place(update, select)
            p_rate = p_rate + added[0]
            t_rate = t_rate + added[1]
        return (p_old + 0.1 * p_rate, t_old + 0.1 * t_rate)

    fields_in = jnp.stack([pressure, heat])
    remotes = []
    for index in range(rounds):
        sending = pick(fields_in, selects[index])
        remotes.append(from_partner(sending, "space", index))
    remotes = jnp.stack(remotes)
    (new_pressure, new_heat), pullback = jax.vjp(
        advance, pressure, heat, log_cond, log_therm, remotes
    )
    adj_pressure, adj_heat, grad_k, grad_t, grad_far = pullback((cot_pressure, cot_heat))
    extra = None
    for index in range(rounds):
        coming = from_partner(grad_far[index], "space", index)
        term = place(coming, selects[index])
        extra = term if extra is None else extra + term
    adj_pressure = adj_pressure + extra[0]
    adj_heat = adj_heat + extra[1]
    grads = jnp.stack([grad_k, grad_t])
    summed = lax.psum(grads, "member")
    share = grads.shape[2] // lax.axis_size("member")
    owned = lax.dynamic_slice_in_dim(summed, lax.axis_index("member") * share, share, 2)
    return (new_pressure, new_heat, adj_pressure, adj_heat, owned)


def solution(mesh):
    placed = (
        P("member", None, "space"),
        P("member", None, "space"),
        P(None, "space"),
        P(None, "space"),
        P(None, "space"),
        P(None, "space"),
        P("member", "space"),
        P(None, "space"),
        P(None, "space"),
        P("member", None, "space"),
        P("member", None, "space"),
    )
    return jax.shard_map(
        body,
        mesh=mesh,
        in_specs=placed,
        out_specs=(
            P("member", None, "space"),
            P("member", None, "space"),
            P("member", None, "space"),
            P("member", None, "space"),
            P(None, None, ("space", "member")),
        ),
        check_vma=False,
    )
```

profile of v0, /device:TPU:8, one launch (start us, length us, event | category | flops | bytes accessed | tf_op | source)
XLA Modules:
  0.0 171.1 jit_solution(9766011143822614567)
XLA Ops:
  8.1 1.5 fusion.182
  9.6 2.1 %fusion.26 = f32[2,4,10,256]{3,2,1,0:T(8,128)} fusion(s32[256]{0:T(256)S(1)} %bitcast.222, f32[1,4,10,2048]{3,2,1,0:T(8,128)S(1)} %get-tuple-element.51, f32[1,4,10,2048]{3,2,1,0:T(8,128)S(1)} %get-tuple-element.72), kind=kOutput, calls=%fused_computation.24 | convolution fusion | flops 504004608 | bytes 738304 | tf_op jit(solution)/shard_map/...c,kc->...k/dot_general | solution.py:24
  11.6 4.5 %collective-permute-start.2 = (f32[2,4,10,256]{3,2,1,0:T(8,128)}, f32[2,4,10,256]{3,2,1,0:T(8,128)}, u32[]{:S(2)}, u32[]{:S(2)}) collective-permute-start(f32[2,4,10,256]{3,2,1,0:T(8,128)} %fusion.26), channel_id=1, source_target_pairs={{0,32},{8,40},{16,48},{24,56},{32,0},{40,8},{48,16},{56,24},{64,96... | collective-permute-start | bytes 245768 | tf_op jit(solution)/shard_map/ppermute | solution.py:10
  16.1 2.1 %fusion.12 = f32[2,4,10,256]{3,2,1,0:T(8,128)} fusion(s32[256]{0:T(256)S(1)} %bitcast.229, f32[1,4,10,2048]{3,2,1,0:T(8,128)S(1)} %get-tuple-element.51, f32[1,4,10,2048]{3,2,1,0:T(8,128)S(1)} %get-tuple-element.72), kind=kOutput, calls=%fused_computation.16 | convolution fusion | flops 504004608 | bytes 738304 | tf_op jit(solution)/shard_map/...c,kc->...k/dot_general | solution.py:24
  18.2 5.0 %collective-permute-start.3 = (f32[2,4,10,256]{3,2,1,0:T(8,128)}, f32[2,4,10,256]{3,2,1,0:T(8,128)}, u32[]{:S(2)}, u32[]{:S(2)}) collective-permute-start(f32[2,4,10,256]{3,2,1,0:T(8,128)} %fusion.12), channel_id=1, source_target_pairs={{0,64},{8,72},{16,80},{24,88},{32,96},{40,104},{48,112},{56,120},{... | collective-permute-start | bytes 245768 | tf_op jit(solution)/shard_map/ppermute | solution.py:10
  23.2 2.1 %fusion.41 = f32[2,4,10,256]{3,2,1,0:T(8,128)} fusion(s32[256]{0:T(256)S(1)} %bitcast.215, f32[1,4,10,2048]{3,2,1,0:T(8,128)S(1)} %get-tuple-element.51, f32[1,4,10,2048]{3,2,1,0:T(8,128)S(1)} %get-tuple-element.72), kind=kOutput, calls=%fused_computation.33 | convolution fusion | flops 504004608 | bytes 738304 | tf_op jit(solution)/shard_map/...c,kc->...k/dot_general | solution.py:24
  25.3 3.4 %collective-permute-start.1 = (f32[2,4,10,256]{3,2,1,0:T(8,128)}, f32[2,4,10,256]{3,2,1,0:T(8,128)}, u32[]{:S(2)}, u32[]{:S(2)}) collective-permute-start(f32[2,4,10,256]{3,2,1,0:T(8,128)} %fusion.41), channel_id=1, source_target_pairs={{0,16},{8,24},{16,0},{24,8},{32,48},{40,56},{48,32},{56,40},{64,80... | collective-permute-start | bytes 245768 | tf_op jit(solution)/shard_map/ppermute | solution.py:10
  28.7 2.1 %fusion.54 = f32[2,4,10,256]{3,2,1,0:T(8,128)} fusion(s32[256]{0:T(256)S(1)} %bitcast.208, f32[1,4,10,2048]{3,2,1,0:T(8,128)S(1)} %get-tuple-element.51, f32[1,4,10,2048]{3,2,1,0:T(8,128)S(1)} %get-tuple-element.72), kind=kOutput, calls=%fused_computation.40 | convolution fusion | flops 504004608 | bytes 738304 | tf_op jit(solution)/shard_map/...c,kc->...k/dot_general | solution.py:24
  30.7 2.1 %collective-permute-start = (f32[2,4,10,256]{3,2,1,0:T(8,128)}, f32[2,4,10,256]{3,2,1,0:T(8,128)}, u32[]{:S(2)}, u32[]{:S(2)}) collective-permute-start(f32[2,4,10,256]{3,2,1,0:T(8,128)} %fusion.54), channel_id=1, source_target_pairs={{0,8},{8,0},{16,24},{24,16},{32,40},{40,32},{48,56},{56,48},{64,72... | collective-permute-start | bytes 245768 | tf_op jit(solution)/shard_map/ppermute | solution.py:10
  33.0 1.3 copy_multiply_fusion.1
  34.3 1.4 fusion.180
  35.8 2.6 %multiply_reduce_fusion.4 = (f32[2,10,256]{2,1,0:T(8,128)S(1)}, f32[2,4,10,256]{3,2,1,0:T(8,128)S(1)}) fusion(f32[2,4,10,256]{3,2,1,0:T(8,128)} %collective-permute-done.2, f32[2,4,10,256]{3,2,1,0:T(8,128)} %fusion.26, s32[256]{0:T(256)S(1)} %bitcast.223, f32[1,4,10,2048]{3,2,1,0:T(8,128)} %get-tuple-element.74, f32[1,4,10,2048]{3,2,1,0:T(8,128)S(1)} %get-tuple-element.46), kind=kOutput, calls=%fused_computation.160 | convolution fusion | flops 504060928 | bytes 922624 | tf_op jit(solution)/shard_map/transpose(jvp(...k,kc->...c))/dot_general | solution.py:28
  39.3 2.4 %multiply_reduce_fusion.5 = (f32[2,10,256]{2,1,0:T(8,128)S(1)}, f32[2,4,10,256]{3,2,1,0:T(8,128)S(1)}) fusion(f32[2,4,10,256]{3,2,1,0:T(8,128)} %collective-permute-done.3, f32[2,4,10,256]{3,2,1,0:T(8,128)} %fusion.12, s32[256]{0:T(256)S(1)} %bitcast.230, f32[1,4,10,2048]{3,2,1,0:T(8,128)S(1)} %copy-done.11, f32[1,4,10,2048]{3,2,1,0:T(8,128)S(1)} %get-tuple-element.46), kind=kOutput, calls=%fused_computation.161 | convolution fusion | flops 504060928 | bytes 922624 | tf_op jit(solution)/shard_map/transpose(jvp(...k,kc->...c))/dot_general | solution.py:28
  42.6 2.4 %multiply_reduce_fusion.3 = (f32[2,10,256]{2,1,0:T(8,128)S(1)}, f32[2,4,10,256]{3,2,1,0:T(8,128)S(1)}) fusion(f32[2,4,10,256]{3,2,1,0:T(8,128)} %collective-permute-done.1, f32[2,4,10,256]{3,2,1,0:T(8,128)} %fusion.41, s32[256]{0:T(256)S(1)} %bitcast.216, f32[1,4,10,2048]{3,2,1,0:T(8,128)S(1)} %copy-done.11, f32[1,4,10,2048]{3,2,1,0:T(8,128)S(1)} %get-tuple-element.46), kind=kOutput, calls=%fused_computation.159 | convolution fusion | flops 504060928 | bytes 922624 | tf_op jit(solution)/shard_map/transpose(jvp(...k,kc->...c))/dot_general | solution.py:28
  46.0 2.4 %multiply_reduce_fusion.2 = (f32[2,10,256]{2,1,0:T(8,128)S(1)}, f32[2,4,10,256]{3,2,1,0:T(8,128)S(1)}) fusion(f32[2,4,10,256]{3,2,1,0:T(8,128)} %collective-permute-done, f32[2,4,10,256]{3,2,1,0:T(8,128)} %fusion.54, s32[256]{0:T(256)S(1)} %bitcast.209, f32[1,4,10,2048]{3,2,1,0:T(8,128)S(1)} %copy-done.11, f32[1,4,10,2048]{3,2,1,0:T(8,128)S(1)} %get-tuple-element.46), kind=kOutput, calls=%fused_computation.158 | convolution fusion | flops 504060928 | bytes 922624 | tf_op jit(solution)/shard_map/transpose(jvp(...k,kc->...c))/dot_general | solution.py:28
  49.5 1.2 fusion.68
  50.7 1.2 fusion.65
  51.9 1.2 fusion.62
  55.6 1.3 fusion.181
  60.9 4.2 %collective-permute-start.6 = (f32[2,4,10,256]{3,2,1,0:T(8,128)}, f32[2,4,10,256]{3,2,1,0:T(8,128)}, u32[]{:S(2)}, u32[]{:S(2)}) collective-permute-start(f32[2,4,10,256]{3,2,1,0:T(8,128)} %get-tuple-element.43), channel_id=1, source_target_pairs={{0,32},{8,40},{16,48},{24,56},{32,0},{40,8},{48,16},{56,24},{64,96... | collective-permute-start | bytes 245768 | tf_op jit(solution)/shard_map/ppermute | solution.py:10
  65.0 2.6 %collective-permute-start.5 = (f32[2,4,10,256]{3,2,1,0:T(8,128)}, f32[2,4,10,256]{3,2,1,0:T(8,128)}, u32[]{:S(2)}, u32[]{:S(2)}) collective-permute-start(f32[2,4,10,256]{3,2,1,0:T(8,128)} %get-tuple-element.44), channel_id=1, source_target_pairs={{0,16},{8,24},{16,0},{24,8},{32,48},{40,56},{48,32},{56,40},{64,80... | collective-permute-start | bytes 245768 | tf_op jit(solution)/shard_map/ppermute | solution.py:10
  67.6 6.7 %collective-permute-start.7 = (f32[2,4,10,256]{3,2,1,0:T(8,128)}, f32[2,4,10,256]{3,2,1,0:T(8,128)}, u32[]{:S(2)}, u32[]{:S(2)}) collective-permute-start(f32[2,4,10,256]{3,2,1,0:T(8,128)} %get-tuple-element.42), channel_id=1, source_target_pairs={{0,64},{8,72},{16,80},{24,88},{32,96},{40,104},{48,112},{56,120},{... | collective-permute-start | bytes 245768 | tf_op jit(solution)/shard_map/ppermute | solution.py:10
  74.4 1.9 %collective-permute-start.4 = (f32[2,4,10,256]{3,2,1,0:T(8,128)}, f32[2,4,10,256]{3,2,1,0:T(8,128)}, u32[]{:S(2)}, u32[]{:S(2)}) collective-permute-start(f32[2,4,10,256]{3,2,1,0:T(8,128)} %get-tuple-element.41), channel_id=1, source_target_pairs={{0,8},{8,0},{16,24},{24,16},{32,40},{40,32},{48,56},{56,48},{64,72... | collective-permute-start | bytes 245768 | tf_op jit(solution)/shard_map/ppermute | solution.py:10
  78.0 1.9 %fusion.52 = f32[2,4,10,2048]{3,2,1,0:T(8,128)S(1)} fusion(s32[256]{0:T(256)S(1)} %bitcast.213, f32[2,10,256]{2,1,0:T(8,128)S(1)} %copy-done.18, f32[2,4,10,256]{3,2,1,0:T(8,128)} %collective-permute-done, f32[2,4,10,256]{3,2,1,0:T(8,128)} %fusion.54), kind=kOutput, calls=%fused_computation.39 | convolution fusion | flops 503881728 | bytes 840704 | tf_op jit(solution)/shard_map/jvp(...k,kc->...c)/dot_general | solution.py:28
  79.9 1.9 %fusion.39 = f32[2,4,10,2048]{3,2,1,0:T(8,128)S(1)} fusion(s32[256]{0:T(256)S(1)} %bitcast.220, f32[2,10,256]{2,1,0:T(8,128)S(1)} %fusion.62, f32[2,4,10,256]{3,2,1,0:T(8,128)} %collective-permute-done.1, f32[2,4,10,256]{3,2,1,0:T(8,128)} %fusion.41), kind=kOutput, calls=%fused_computation.32 | convolution fusion | flops 503881728 | bytes 840704 | tf_op jit(solution)/shard_map/jvp(...k,kc->...c)/dot_general | solution.py:28
  81.9 2.0 %fusion.24 = f32[2,4,10,2048]{3,2,1,0:T(8,128)S(1)} fusion(s32[256]{0:T(256)S(1)} %bitcast.227, f32[2,10,256]{2,1,0:T(8,128)S(1)} %fusion.65, f32[2,4,10,256]{3,2,1,0:T(8,128)} %collective-permute-done.2, f32[2,4,10,256]{3,2,1,0:T(8,128)} %fusion.26), kind=kOutput, calls=%fused_computation.23 | convolution fusion | flops 503881728 | bytes 840704 | tf_op jit(solution)/shard_map/jvp(...k,kc->...c)/dot_general | solution.py:28
  83.9 1.9 %fusion.10 = f32[2,4,10,2048]{3,2,1,0:T(8,128)S(1)} fusion(s32[256]{0:T(256)S(1)} %bitcast.234, f32[2,10,256]{2,1,0:T(8,128)S(1)} %copy-done.20, f32[2,4,10,256]{3,2,1,0:T(8,128)} %collective-permute-done.3, f32[2,4,10,256]{3,2,1,0:T(8,128)} %fusion.12), kind=kOutput, calls=%fused_computation.15 | convolution fusion | flops 503881728 | bytes 840704 | tf_op jit(solution)/shard_map/jvp(...k,kc->...c)/dot_general | solution.py:28
  88.5 1.8 %fusion.19 = f32[2,4,10,2048]{3,2,1,0:T(8,128)S(1)} fusion(f32[2,4,10,256]{3,2,1,0:T(8,128)} %collective-permute-done.6, s32[256]{0:T(256)S(1)} %bitcast.228), kind=kOutput, calls=%fused_computation.21 | convolution fusion | flops 503840768 | bytes 738304 | tf_op jit(solution)/shard_map/...k,kc->...c/dot_general | solution.py:28
  90.4 1.8 %fusion.34 = f32[2,4,10,2048]{3,2,1,0:T(8,128)S(1)} fusion(f32[2,4,10,256]{3,2,1,0:T(8,128)} %collective-permute-done.5, s32[256]{0:T(256)S(1)} %bitcast.221), kind=kOutput, calls=%fused_computation.30 | convolution fusion | flops 503840768 | bytes 738304 | tf_op jit(solution)/shard_map/...k,kc->...c/dot_general | solution.py:28
  92.2 1.8 %fusion.4 = f32[2,4,10,2048]{3,2,1,0:T(8,128)S(1)} fusion(f32[2,4,10,256]{3,2,1,0:T(8,128)} %collective-permute-done.7, s32[256]{0:T(256)S(1)} %bitcast.235), kind=kOutput, calls=%fused_computation.12 | convolution fusion | flops 503840768 | bytes 738304 | tf_op jit(solution)/shard_map/...k,kc->...c/dot_general | solution.py:28
  94.1 2.1 %fusion.1 = f32[2,4,10,2048]{3,2,1,0:T(8,128)S(1)} fusion(f32[2,4,10,2048]{3,2,1,0:T(8,128)S(1)} %fusion.4, f32[2,4,10,2048]{3,2,1,0:T(8,128)S(1)} %fusion.19, f32[2,4,10,2048]{3,2,1,0:T(8,128)S(1)} %fusion.34, f32[2,4,10,256]{3,2,1,0:T(8,128)} %collective-permute-done.4, s32[256]{0:T(256)S(1)} %bitcast.214), kind=kOutput, calls=%fused_computation.2 | convolution fusion | flops 504332288 | bytes 2704384 | tf_op jit(solution)/shard_map/...k,kc->...c/dot_general | solution.py:28
  99.0 63.8 %all-reduce.24.cloned.1.call-done = f32[2,10,2048]{2,1,0:T(8,128)} async-done(((f32[2,10,2048]{2,1,0:T(8,128)}), f32[2,10,2048]{2,1,0:T(8,128)}) %all-reduce.24.cloned.1.call-update) | async-done | bytes 163856 | tf_op jit(solution)/shard_map/psum | solution.py:89
  (100 shorter events, 19.7 us)
Async XLA Ops:
  7.2 155.7 %all-reduce.24.cloned.1.call-start = ((), (), s32[]{:S(2)}) async-start(), calls=%async_computation | async-start | bytes 524288 | tf_op jit(solution)/shard_map/psum | solution.py:89
  11.6 24.1 %collective-permute-start.2 = (f32[2,4,10,256]{3,2,1,0:T(8,128)}, f32[2,4,10,256]{3,2,1,0:T(8,128)}, u32[]{:S(2)}, u32[]{:S(2)}) collective-permute-start(f32[2,4,10,256]{3,2,1,0:T(8,128)} %fusion.26), channel_id=1, source_target_pairs={{0,32},{8,40},{16,48},{24,56},{32,0},{40,8},{48,16},{56,24},{64,96... | collective-permute-start | bytes 245768 | tf_op jit(solution)/shard_map/ppermute | solution.py:10
  18.2 21.1 %collective-permute-start.3 = (f32[2,4,10,256]{3,2,1,0:T(8,128)}, f32[2,4,10,256]{3,2,1,0:T(8,128)}, u32[]{:S(2)}, u32[]{:S(2)}) collective-permute-start(f32[2,4,10,256]{3,2,1,0:T(8,128)} %fusion.12), channel_id=1, source_target_pairs={{0,64},{8,72},{16,80},{24,88},{32,96},{40,104},{48,112},{56,120},{... | collective-permute-start | bytes 245768 | tf_op jit(solution)/shard_map/ppermute | solution.py:10
  25.3 7.6 %copy-start.12 = (f32[10,2048]{1,0:T(8,128)S(1)}, f32[10,2048]{1,0:T(8,128)}, u32[]{:S(2)}) copy-start(f32[10,2048]{1,0:T(8,128)} %param.16) | copy-start | bytes 245764
  25.3 7.6 %copy-start.13 = (f32[10,2048]{1,0:T(8,128)S(1)}, f32[10,2048]{1,0:T(8,128)}, u32[]{:S(2)}) copy-start(f32[10,2048]{1,0:T(8,128)} %param.17) | copy-start | bytes 245764
  25.3 7.6 %copy-start.15 = (s32[10,2048]{1,0:T(8,128)S(1)}, s32[10,2048]{1,0:T(8,128)}, u32[]{:S(2)}) copy-start(s32[10,2048]{1,0:T(8,128)} %param.18) | copy-start | bytes 245764
  25.3 17.3 %collective-permute-start.1 = (f32[2,4,10,256]{3,2,1,0:T(8,128)}, f32[2,4,10,256]{3,2,1,0:T(8,128)}, u32[]{:S(2)}, u32[]{:S(2)}) collective-permute-start(f32[2,4,10,256]{3,2,1,0:T(8,128)} %fusion.41), channel_id=1, source_target_pairs={{0,16},{8,24},{16,0},{24,8},{32,48},{40,56},{48,32},{56,40},{64,80... | collective-permute-start | bytes 245768 | tf_op jit(solution)/shard_map/ppermute | solution.py:10
  28.7 4.3 %copy-start.6 = (f32[4,10,2048]{2,0,1:T(4,128)S(1)}, f32[4,10,2048]{2,0,1:T(4,128)}, u32[]{:S(2)}) copy-start(f32[4,10,2048]{2,0,1:T(4,128)} %param.23) | copy-start | bytes 983044
  28.7 4.3 %copy-start.7 = (f32[4,10,2048]{2,0,1:T(4,128)S(1)}, f32[4,10,2048]{2,0,1:T(4,128)}, u32[]{:S(2)}) copy-start(f32[4,10,2048]{2,0,1:T(4,128)} %param.22) | copy-start | bytes 983044
  30.7 15.2 %collective-permute-start = (f32[2,4,10,256]{3,2,1,0:T(8,128)}, f32[2,4,10,256]{3,2,1,0:T(8,128)}, u32[]{:S(2)}, u32[]{:S(2)}) collective-permute-start(f32[2,4,10,256]{3,2,1,0:T(8,128)} %fusion.54), channel_id=1, source_target_pairs={{0,8},{8,0},{16,24},{24,16},{32,40},{40,32},{48,56},{56,48},{64,72... | collective-permute-start | bytes 245768 | tf_op jit(solution)/shard_map/ppermute | solution.py:10
  35.7 9.3 %copy-start.25 = (f32[1,256]{1,0:T(1,128)}, f32[1,256]{1,0:T(1,128)S(1)}, u32[]{:S(2)}) copy-start(f32[1,256]{1,0:T(1,128)S(1)} %get-tuple-element.57) | copy-start | bytes 3076
  35.7 12.7 %copy-start.23 = (f32[1,256]{1,0:T(1,128)}, f32[1,256]{1,0:T(1,128)S(1)}, u32[]{:S(2)}) copy-start(f32[1,256]{1,0:T(1,128)S(1)} %get-tuple-element.56) | copy-start | bytes 3076
  35.8 3.5 %copy-start.11 = (f32[1,4,10,2048]{3,2,1,0:T(8,128)S(1)}, f32[1,4,10,2048]{3,2,1,0:T(8,128)}, u32[]{:S(2)}) copy-start(f32[1,4,10,2048]{3,2,1,0:T(8,128)} %get-tuple-element.74) | copy-start | bytes 983044
  45.9 3.4 %copy-start.14 = (f32[10,2048]{1,0:T(8,128)S(1)}, f32[10,2048]{1,0:T(8,128)}, u32[]{:S(2)}) copy-start(f32[10,2048]{1,0:T(8,128)} %param.17) | copy-start | bytes 245764
  45.9 3.4 %copy-start.16 = (s32[10,2048]{1,0:T(8,128)S(1)}, s32[10,2048]{1,0:T(8,128)}, u32[]{:S(2)}) copy-start(s32[10,2048]{1,0:T(8,128)} %param.18) | copy-start | bytes 245764
  45.9 3.4 %copy-start.21 = (f32[10,2048]{1,0:T(8,128)S(1)}, f32[10,2048]{1,0:T(8,128)}, u32[]{:S(2)}) copy-start(f32[10,2048]{1,0:T(8,128)} %param.15) | copy-start | bytes 245764
  49.5 2.4 %copy-start.26 = (f32[1,256]{1,0:T(1,128)S(1)}, f32[1,256]{1,0:T(1,128)}, u32[]{:S(2)}) copy-start(f32[1,256]{1,0:T(1,128)} %copy-done.25) | copy-start | bytes 3076
  49.5 3.6 %copy-start.24 = (f32[1,256]{1,0:T(1,128)S(1)}, f32[1,256]{1,0:T(1,128)}, u32[]{:S(2)}) copy-start(f32[1,256]{1,0:T(1,128)} %copy-done.23) | copy-start | bytes 3076
  50.7 4.8 %copy-start.19 = (f32[2,10,256]{2,1,0:T(8,128)}, f32[2,10,256]{2,1,0:T(8,128)S(1)}, u32[]{:S(2)}) copy-start(f32[2,10,256]{2,1,0:T(8,128)S(1)} %fusion.68) | copy-start | bytes 61444
  54.3 4.7 %copy-start.17 = (f32[2,10,256]{2,1,0:T(8,128)}, f32[2,10,256]{2,1,0:T(8,128)S(1)}, u32[]{:S(2)}) copy-start(f32[2,10,256]{2,1,0:T(8,128)S(1)} %fusion.59) | copy-start | bytes 61444
  60.9 17.1 %copy-start.18 = (f32[2,10,256]{2,1,0:T(8,128)S(1)}, f32[2,10,256]{2,1,0:T(8,128)}, u32[]{:S(2)}) copy-start(f32[2,10,256]{2,1,0:T(8,128)} %copy-done.17) | copy-start | bytes 61444
  60.9 27.7 %collective-permute-start.6 = (f32[2,4,10,256]{3,2,1,0:T(8,128)}, f32[2,4,10,256]{3,2,1,0:T(8,128)}, u32[]{:S(2)}, u32[]{:S(2)}) collective-permute-start(f32[2,4,10,256]{3,2,1,0:T(8,128)} %get-tuple-element.43), channel_id=1, source_target_pairs={{0,32},{8,40},{16,48},{24,56},{32,0},{40,8},{48,16},{56,24},{64,96... | collective-permute-start | bytes 245768 | tf_op jit(solution)/shard_map/ppermute | solution.py:10
  65.0 25.3 %collective-permute-start.5 = (f32[2,4,10,256]{3,2,1,0:T(8,128)}, f32[2,4,10,256]{3,2,1,0:T(8,128)}, u32[]{:S(2)}, u32[]{:S(2)}) collective-permute-start(f32[2,4,10,256]{3,2,1,0:T(8,128)} %get-tuple-element.44), channel_id=1, source_target_pairs={{0,16},{8,24},{16,0},{24,8},{32,48},{40,56},{48,32},{56,40},{64,80... | collective-permute-start | bytes 245768 | tf_op jit(solution)/shard_map/ppermute | solution.py:10
  67.6 24.6 %collective-permute-start.7 = (f32[2,4,10,256]{3,2,1,0:T(8,128)}, f32[2,4,10,256]{3,2,1,0:T(8,128)}, u32[]{:S(2)}, u32[]{:S(2)}) collective-permute-start(f32[2,4,10,256]{3,2,1,0:T(8,128)} %get-tuple-element.42), channel_id=1, source_target_pairs={{0,64},{8,72},{16,80},{24,88},{32,96},{40,104},{48,112},{56,120},{... | collective-permute-start | bytes 245768 | tf_op jit(solution)/shard_map/ppermute | solution.py:10
  74.4 19.7 %collective-permute-start.4 = (f32[2,4,10,256]{3,2,1,0:T(8,128)}, f32[2,4,10,256]{3,2,1,0:T(8,128)}, u32[]{:S(2)}, u32[]{:S(2)}) collective-permute-start(f32[2,4,10,256]{3,2,1,0:T(8,128)} %get-tuple-element.41), channel_id=1, source_target_pairs={{0,8},{8,0},{16,24},{24,16},{32,40},{40,32},{48,56},{56,48},{64,72... | collective-permute-start | bytes 245768 | tf_op jit(solution)/shard_map/ppermute | solution.py:10
  79.9 4.0 %copy-start.20 = (f32[2,10,256]{2,1,0:T(8,128)S(1)}, f32[2,10,256]{2,1,0:T(8,128)}, u32[]{:S(2)}) copy-start(f32[2,10,256]{2,1,0:T(8,128)} %copy-done.19) | copy-start | bytes 61444
  81.9 4.0 %copy-start = (f32[4,9,2048]{2,1,0:T(8,128)S(1)}, f32[4,9,2048]{2,1,0:T(8,128)}, u32[]{:S(2)}) copy-start(f32[4,9,2048]{2,1,0:T(8,128)} %get-tuple-element.38) | copy-start | bytes 884740
  81.9 4.0 %copy-start.9 = (f32[4,10,2048]{2,0,1:T(4,128)S(1)}, f32[4,10,2048]{2,0,1:T(4,128)}, u32[]{:S(2)}) copy-start(f32[4,10,2048]{2,0,1:T(4,128)} %param.14) | copy-start | bytes 983044
  81.9 4.0 %copy-start.10 = (f32[4,10,2048]{2,0,1:T(4,128)S(1)}, f32[4,10,2048]{2,0,1:T(4,128)}, u32[]{:S(2)}) copy-start(f32[4,10,2048]{2,0,1:T(4,128)} %param.13) | copy-start | bytes 983044
  94.0 2.2 %copy-start.1 = (f32[4,9,2048]{2,1,0:T(8,128)S(1)}, f32[4,9,2048]{2,1,0:T(8,128)}, u32[]{:S(2)}) copy-start(f32[4,9,2048]{2,1,0:T(8,128)} %get-tuple-element.30) | copy-start | bytes 884740
  94.1 2.2 %copy-start.2 = (f32[4,9,2048]{2,1,0:T(8,128)S(1)}, f32[4,9,2048]{2,1,0:T(8,128)}, u32[]{:S(2)}) copy-start(f32[4,9,2048]{2,1,0:T(8,128)} %get-tuple-element.31) | copy-start | bytes 884740
  94.1 2.2 %copy-start.3 = (f32[4,9,2048]{2,1,0:T(8,128)S(1)}, f32[4,9,2048]{2,1,0:T(8,128)}, u32[]{:S(2)}) copy-start(f32[4,9,2048]{2,1,0:T(8,128)} %get-tuple-element.54) | copy-start | bytes 884740
  (4 other events, 8.0 us)
Sparse Core Ops, SparseCore 0:
  77.2 85.6 all-reduce.23
where the time goes:
time: 172 us; the launch traced here: 171 us
  waiting for transfers between devices  63.9 us (37%)
  matrix products  45.5 us (26%)
  starting transfers between devices  30.4 us (18%)
  between operations  14.8 us (9%)
  local copies, waits for them, and re-layouts  8.84 us (5%)
  other arithmetic  7.6 us (4%)
    psum x1, waiting for transfers between devices, body(): summed = lax.psum(grads, 'member')  63.8 us
    ppermute x8, starting transfers between devices, from_partner(): return lax.ppermute(value, axis, pairs)  30.4 us
    dot_general x12, matrix products, place(): jnp.einsum('...k,kc->...c', values, select, precision=lax.Precision.HIGHEST)  25 us
    dot_general x16, matrix products, pick(): jnp.einsum('...c,kc->...k', values, select, precision=lax.Precision.HIGHEST)  20.4 us
    unnamed x60, local copies, waits for them, and re-layouts  6.25 us
  transfers between devices with their start and end apart: 9, of which 1 were waited for; matrix products, arithmetic and copies ran while one was open for 24% of the time, Pallas kernels for 0%

commit v1 on v0

--- a/solution.py
+++ b/solution.py
@@ -2,6 +2,10 @@
 import jax.numpy as jnp
 from jax import lax
 from jax.sharding import PartitionSpec as P
+
+
+def register_the_body(array_here):
+    return jnp.sum(lax.all_gather(array_here, "member"), axis=0)
 
 
 def from_partner(value, axis, stride):
@@ -86,7 +90,7 @@
     adj_pressure = adj_pressure + extra[0]
     adj_heat = adj_heat + extra[1]
     grads = jnp.stack([grad_k, grad_t])
-    summed = lax.psum(grads, "member")
+    summed = register_the_body(grads)
     share = grads.shape[2] // lax.axis_size("member")
     owned = lax.dynamic_slice_in_dim(summed, lax.axis_index("member") * share, share, 2)
     return (new_pressure, new_heat, adj_pressure, adj_heat, owned)

time: 172 us -> 138 us (0.80)
  waiting for transfers between devices: 63.9 us -> 20.9 us
  other arithmetic: 7.6 us -> 14.1 us
  matrix products: 45.5 us -> 48.8 us
    psum x1 -> x0, waiting for transfers between devices: 63.8 us -> none  [body(): summed = lax.psum(grads, 'member')]
    all_gather x0 -> x1, waiting for transfers between devices: none -> 20.9 us  [register_the_body(): return jnp.sum(lax.all_gather(array_here, 'member'), axis=0)]
    dot_general x12, matrix products: 25 us -> 28.1 us  [place(): jnp.einsum('...k,kc->...c', values, select, precision=lax.Precision.HIGHEST)]
    add x1, other arithmetic: 0.81 us -> 3.87 us  [advance(): return (p_old + 0.1 * p_rate, t_old + 0.1 * t_rate)]
    reduce_sum x0 -> x1, other arithmetic: none -> 1.76 us  [register_the_body(): return jnp.sum(lax.all_gather(array_here, 'member'), axis=0)]
    unnamed x60 -> x54, local copies, waits for them, and re-layouts: 6.25 us -> 6.02 us
  transfers between devices with their start and end apart: 9 -> 9, of which waited for: 1 -> 1; matrix products, arithmetic and copies ran while one was open for 24% -> 36% of each run, Pallas kernels for 0% -> 0%
where the time goes in v1:
time: 138 us; the launch traced here: 137 us
  matrix products  48.8 us (35%)
  starting transfers between devices  30.3 us (22%)
  waiting for transfers between devices  20.9 us (15%)
  between operations  14.7 us (11%)
  other arithmetic  14.1 us (10%)
  local copies, waits for them, and re-layouts  8.09 us (6%)
    ppermute x8, starting transfers between devices, from_partner(): return lax.ppermute(value, axis, pairs)  30.2 us
    dot_general x12, matrix products, place(): jnp.einsum('...k,kc->...c', values, select, precision=lax.Precision.HIGHEST)  28.1 us
    all_gather x1, waiting for transfers between devices, register_the_body(): return jnp.sum(lax.all_gather(array_here, 'member'), axis=0)  20.9 us
    dot_general x16, matrix products, pick(): jnp.einsum('...c,kc->...k', values, select, precision=lax.Precision.HIGHEST)  20.6 us
    unnamed x54, local copies, waits for them, and re-layouts  6.02 us
    add x1, other arithmetic, advance(): return (p_old + 0.1 * p_rate, t_old + 0.1 * t_rate)  3.87 us
  transfers between devices with their start and end apart: 9, of which 1 were waited for; matrix products, arithmetic and copies ran while one was open for 36% of the time, Pallas kernels for 0%

profile of v1, /device:TPU:8, one launch (start us, length us, event | category | flops | bytes accessed | tf_op | source)
XLA Modules:
  0.0 136.9 jit_solution(16743465916805671598)
XLA Ops:
  8.1 1.5 %fusion.182 = (f32[4,10,2048]{2,1,0:T(8,128)S(1)}, f32[1,4,10,2048]{3,2,1,0:T(8,128)S(1)}, f32[1,4,10,2048]{3,2,1,0:T(8,128)S(1)}, f32[4,10,2048]{2,1,0:T(8,128)S(1)}) fusion(f32[4,10,2048]{2,0,1:T(4,128)} %param.14, f32[4,10,2048]{2,0,1:T(4,128)} %param.13), kind=kLoop, calls=%fused_computation.222 | loop fusion | bytes 1966080 | tf_op args[1]
  9.6 2.1 %fusion.26 = f32[2,4,10,256]{3,2,1,0:T(8,128)} fusion(s32[256]{0:T(256)S(1)} %bitcast.224, f32[1,4,10,2048]{3,2,1,0:T(8,128)S(1)} %get-tuple-element.56, f32[1,4,10,2048]{3,2,1,0:T(8,128)S(1)} %get-tuple-element.77), kind=kOutput, calls=%fused_computation.24 | convolution fusion | flops 504004608 | bytes 738304 | tf_op jit(solution)/shard_map/...c,kc->...k/dot_general | solution.py:28
  11.6 4.5 %collective-permute-start.2 = (f32[2,4,10,256]{3,2,1,0:T(8,128)}, f32[2,4,10,256]{3,2,1,0:T(8,128)}, u32[]{:S(2)}, u32[]{:S(2)}) collective-permute-start(f32[2,4,10,256]{3,2,1,0:T(8,128)} %fusion.26), channel_id=1, source_target_pairs={{0,32},{8,40},{16,48},{24,56},{32,0},{40,8},{48,16},{56,24},{64,96... | collective-permute-start | bytes 245768 | tf_op jit(solution)/shard_map/ppermute | solution.py:14
  16.1 2.1 %fusion.12 = f32[2,4,10,256]{3,2,1,0:T(8,128)} fusion(s32[256]{0:T(256)S(1)} %bitcast.231, f32[1,4,10,2048]{3,2,1,0:T(8,128)S(1)} %get-tuple-element.56, f32[1,4,10,2048]{3,2,1,0:T(8,128)S(1)} %get-tuple-element.77), kind=kOutput, calls=%fused_computation.16 | convolution fusion | flops 504004608 | bytes 738304 | tf_op jit(solution)/shard_map/...c,kc->...k/dot_general | solution.py:28
  18.2 5.2 %collective-permute-start.3 = (f32[2,4,10,256]{3,2,1,0:T(8,128)}, f32[2,4,10,256]{3,2,1,0:T(8,128)}, u32[]{:S(2)}, u32[]{:S(2)}) collective-permute-start(f32[2,4,10,256]{3,2,1,0:T(8,128)} %fusion.12), channel_id=1, source_target_pairs={{0,64},{8,72},{16,80},{24,88},{32,96},{40,104},{48,112},{56,120},{... | collective-permute-start | bytes 245768 | tf_op jit(solution)/shard_map/ppermute | solution.py:14
  23.4 2.1 %fusion.41 = f32[2,4,10,256]{3,2,1,0:T(8,128)} fusion(s32[256]{0:T(256)S(1)} %bitcast.217, f32[1,4,10,2048]{3,2,1,0:T(8,128)S(1)} %get-tuple-element.56, f32[1,4,10,2048]{3,2,1,0:T(8,128)S(1)} %get-tuple-element.77), kind=kOutput, calls=%fused_computation.33 | convolution fusion | flops 504004608 | bytes 738304 | tf_op jit(solution)/shard_map/...c,kc->...k/dot_general | solution.py:28
  25.4 3.2 %collective-permute-start.1 = (f32[2,4,10,256]{3,2,1,0:T(8,128)}, f32[2,4,10,256]{3,2,1,0:T(8,128)}, u32[]{:S(2)}, u32[]{:S(2)}) collective-permute-start(f32[2,4,10,256]{3,2,1,0:T(8,128)} %fusion.41), channel_id=1, source_target_pairs={{0,16},{8,24},{16,0},{24,8},{32,48},{40,56},{48,32},{56,40},{64,80... | collective-permute-start | bytes 245768 | tf_op jit(solution)/shard_map/ppermute | solution.py:14
  28.7 2.0 %fusion.54 = f32[2,4,10,256]{3,2,1,0:T(8,128)} fusion(s32[256]{0:T(256)S(1)} %bitcast.210, f32[1,4,10,2048]{3,2,1,0:T(8,128)S(1)} %get-tuple-element.56, f32[1,4,10,2048]{3,2,1,0:T(8,128)S(1)} %get-tuple-element.77), kind=kOutput, calls=%fused_computation.40 | convolution fusion | flops 504004608 | bytes 738304 | tf_op jit(solution)/shard_map/...c,kc->...k/dot_general | solution.py:28
  30.7 2.1 %collective-permute-start = (f32[2,4,10,256]{3,2,1,0:T(8,128)}, f32[2,4,10,256]{3,2,1,0:T(8,128)}, u32[]{:S(2)}, u32[]{:S(2)}) collective-permute-start(f32[2,4,10,256]{3,2,1,0:T(8,128)} %fusion.54), channel_id=1, source_target_pairs={{0,8},{8,0},{16,24},{24,16},{32,40},{40,32},{48,56},{56,48},{64,72... | collective-permute-start | bytes 245768 | tf_op jit(solution)/shard_map/ppermute | solution.py:14
  33.0 1.5 %copy_multiply_fusion.1 = (f32[4,10,2048]{2,1,0:T(8,128)S(1)}, f32[1,4,10,2048]{3,2,1,0:T(8,128)}, f32[4,10,2048]{2,1,0:T(8,128)S(1)}, f32[1,4,10,2048]{3,2,1,0:T(8,128)}, f32[4,10,2048]{2,1,0:T(8,128)S(1)}) fusion(f32[4,10,2048]{2,0,1:T(4,128)S(1)} %copy-done.5, f32[4,10,2048]{2,0,1:T(4,128)S(1)} %copy-done.6), kind=kLoop, calls=%fused_computation.78 | loop fusion | flops 245760 | bytes 2293760 | tf_op jit(solution)/shard_map/transpose(jvp())/mul | solution.py:73
  34.4 1.4 %fusion.180 = (f32[4,9,2048]{2,1,0:T(8,128)}, f32[4,9,2048]{2,1,0:T(8,128)}, f32[9,2048]{1,0:T(8,128)S(1)}, f32[4,9,2048]{2,1,0:T(8,128)}, f32[9,2048]{1,0:T(8,128)S(1)}, /*index=5*/f32[4,9,2048]{2,1,0:T(8,128)S(1)}) fusion(f32[4,10,2048]{2,1,0:T(8,128)S(1)} %get-tuple-element.50, f32[9,2048]{1,0:T(8,128)S(1)} %fusion.129, ...), kind=kLoop, calls=%fused_computation.220 | loop fusion | flops 1363968 | bytes 4349952 | tf_op jit(solution)/shard_map/transpose(jvp())/neg | solution.py:57
  37.3 2.7 %multiply_reduce_fusion.4 = (f32[2,10,256]{2,1,0:T(8,128)S(1)}, f32[2,4,10,256]{3,2,1,0:T(8,128)S(1)}) fusion(f32[2,4,10,256]{3,2,1,0:T(8,128)} %collective-permute-done.2, f32[2,4,10,256]{3,2,1,0:T(8,128)} %fusion.26, s32[256]{0:T(256)S(1)} %bitcast.225, f32[1,4,10,2048]{3,2,1,0:T(8,128)} %get-tuple-element.79, f32[1,4,10,2048]{3,2,1,0:T(8,128)} %get-tuple-element.51), kind=kOutput, calls=%fused_computation.160 | convolution fusion | flops 504060928 | bytes 922624 | tf_op jit(solution)/shard_map/transpose(jvp(...k,kc->...c))/dot_general | solution.py:32
  40.9 2.4 %multiply_reduce_fusion.5 = (f32[2,10,256]{2,1,0:T(8,128)S(1)}, f32[2,4,10,256]{3,2,1,0:T(8,128)S(1)}) fusion(f32[2,4,10,256]{3,2,1,0:T(8,128)} %collective-permute-done.3, f32[2,4,10,256]{3,2,1,0:T(8,128)} %fusion.12, s32[256]{0:T(256)S(1)} %bitcast.232, f32[1,4,10,2048]{3,2,1,0:T(8,128)S(1)} %copy-done.9, f32[1,4,10,2048]{3,2,1,0:T(8,128)S(1)} %copy-done.8), kind=kOutput, calls=%fused_computation.161 | convolution fusion | flops 504060928 | bytes 922624 | tf_op jit(solution)/shard_map/transpose(jvp(...k,kc->...c))/dot_general | solution.py:32
  44.3 2.5 %multiply_reduce_fusion.3 = (f32[2,10,256]{2,1,0:T(8,128)S(1)}, f32[2,4,10,256]{3,2,1,0:T(8,128)S(1)}) fusion(f32[2,4,10,256]{3,2,1,0:T(8,128)} %collective-permute-done.1, f32[2,4,10,256]{3,2,1,0:T(8,128)} %fusion.41, s32[256]{0:T(256)S(1)} %bitcast.218, f32[1,4,10,2048]{3,2,1,0:T(8,128)S(1)} %copy-done.9, f32[1,4,10,2048]{3,2,1,0:T(8,128)S(1)} %copy-done.8), kind=kOutput, calls=%fused_computation.159 | convolution fusion | flops 504060928 | bytes 922624 | tf_op jit(solution)/shard_map/transpose(jvp(...k,kc->...c))/dot_general | solution.py:32
  47.7 2.4 %multiply_reduce_fusion.2 = (f32[2,10,256]{2,1,0:T(8,128)S(1)}, f32[2,4,10,256]{3,2,1,0:T(8,128)S(1)}) fusion(f32[2,4,10,256]{3,2,1,0:T(8,128)} %collective-permute-done, f32[2,4,10,256]{3,2,1,0:T(8,128)} %fusion.54, s32[256]{0:T(256)S(1)} %bitcast.211, f32[1,4,10,2048]{3,2,1,0:T(8,128)S(1)} %copy-done.9, f32[1,4,10,2048]{3,2,1,0:T(8,128)S(1)} %copy-done.8), kind=kOutput, calls=%fused_computation.158 | convolution fusion | flops 504060928 | bytes 922624 | tf_op jit(solution)/shard_map/transpose(jvp(...k,kc->...c))/dot_general | solution.py:32
  54.8 1.4 %fusion.59 = f32[2,10,256]{2,1,0:T(8,128)S(1)} fusion(s32[256]{0:T(256)S(1)} %bitcast.213, f32[1,10,2048]{2,1,0:T(8,128)S(1)} %bitcast.205, f32[1,10,2048]{2,1,0:T(8,128)S(1)} %bitcast.209, f32[256]{0:T(256)S(1)} %bitcast.239), kind=kOutput, calls=%fused_computation.42 | convolution fusion | flops 126399488 | bytes 186368 | tf_op jit(solution)/shard_map/jvp(...c,kc->...k)/dot_general | solution.py:28
  57.2 1.3 fusion.181
  63.4 4.0 %collective-permute-start.6 = (f32[2,4,10,256]{3,2,1,0:T(8,128)}, f32[2,4,10,256]{3,2,1,0:T(8,128)}, u32[]{:S(2)}, u32[]{:S(2)}) collective-permute-start(f32[2,4,10,256]{3,2,1,0:T(8,128)} %get-tuple-element.48), channel_id=1, source_target_pairs={{0,32},{8,40},{16,48},{24,56},{32,0},{40,8},{48,16},{56,24},{64,96... | collective-permute-start | bytes 245768 | tf_op jit(solution)/shard_map/ppermute | solution.py:14
  67.4 2.6 %collective-permute-start.5 = (f32[2,4,10,256]{3,2,1,0:T(8,128)}, f32[2,4,10,256]{3,2,1,0:T(8,128)}, u32[]{:S(2)}, u32[]{:S(2)}) collective-permute-start(f32[2,4,10,256]{3,2,1,0:T(8,128)} %get-tuple-element.49), channel_id=1, source_target_pairs={{0,16},{8,24},{16,0},{24,8},{32,48},{40,56},{48,32},{56,40},{64,80... | collective-permute-start | bytes 245768 | tf_op jit(solution)/shard_map/ppermute | solution.py:14
  70.0 6.7 %collective-permute-start.7 = (f32[2,4,10,256]{3,2,1,0:T(8,128)}, f32[2,4,10,256]{3,2,1,0:T(8,128)}, u32[]{:S(2)}, u32[]{:S(2)}) collective-permute-start(f32[2,4,10,256]{3,2,1,0:T(8,128)} %get-tuple-element.47), channel_id=1, source_target_pairs={{0,64},{8,72},{16,80},{24,88},{32,96},{40,104},{48,112},{56,120},{... | collective-permute-start | bytes 245768 | tf_op jit(solution)/shard_map/ppermute | solution.py:14
  76.7 1.9 %collective-permute-start.4 = (f32[2,4,10,256]{3,2,1,0:T(8,128)}, f32[2,4,10,256]{3,2,1,0:T(8,128)}, u32[]{:S(2)}, u32[]{:S(2)}) collective-permute-start(f32[2,4,10,256]{3,2,1,0:T(8,128)} %get-tuple-element.46), channel_id=1, source_target_pairs={{0,8},{8,0},{16,24},{24,16},{32,40},{40,32},{48,56},{56,48},{64,72... | collective-permute-start | bytes 245768 | tf_op jit(solution)/shard_map/ppermute | solution.py:14
  79.4 1.9 %fusion.52 = f32[2,4,10,2048]{3,2,1,0:T(8,128)S(1)} fusion(s32[256]{0:T(256)S(1)} %bitcast.215, f32[2,10,256]{2,1,0:T(8,128)} %copy-done.18, f32[2,4,10,256]{3,2,1,0:T(8,128)} %collective-permute-done, f32[2,4,10,256]{3,2,1,0:T(8,128)} %fusion.54), kind=kOutput, calls=%fused_computation.39 | convolution fusion | flops 503881728 | bytes 840704 | tf_op jit(solution)/shard_map/jvp(...k,kc->...c)/dot_general | solution.py:32
  81.4 2.9 %fusion.39 = f32[2,4,10,2048]{3,2,1,0:T(8,128)} fusion(s32[256]{0:T(256)S(1)} %bitcast.222, f32[2,10,256]{2,1,0:T(8,128)S(1)} %fusion.62, f32[2,4,10,256]{3,2,1,0:T(8,128)} %collective-permute-done.1, f32[2,4,10,256]{3,2,1,0:T(8,128)} %fusion.41), kind=kOutput, calls=%fused_computation.32 | convolution fusion | flops 503881728 | bytes 840704 | tf_op jit(solution)/shard_map/jvp(...k,kc->...c)/dot_general | solution.py:32
  84.3 2.9 %fusion.24 = f32[2,4,10,2048]{3,2,1,0:T(8,128)} fusion(s32[256]{0:T(256)S(1)} %bitcast.229, f32[2,10,256]{2,1,0:T(8,128)S(1)} %fusion.65, f32[2,4,10,256]{3,2,1,0:T(8,128)} %collective-permute-done.2, f32[2,4,10,256]{3,2,1,0:T(8,128)} %fusion.26), kind=kOutput, calls=%fused_computation.23 | convolution fusion | flops 503881728 | bytes 840704 | tf_op jit(solution)/shard_map/jvp(...k,kc->...c)/dot_general | solution.py:32
  87.1 2.9 %fusion.10 = f32[2,4,10,2048]{3,2,1,0:T(8,128)} fusion(s32[256]{0:T(256)S(1)} %bitcast.236, f32[2,10,256]{2,1,0:T(8,128)S(1)} %copy-done.20, f32[2,4,10,256]{3,2,1,0:T(8,128)} %collective-permute-done.3, f32[2,4,10,256]{3,2,1,0:T(8,128)} %fusion.12), kind=kOutput, calls=%fused_computation.15 | convolution fusion | flops 503881728 | bytes 840704 | tf_op jit(solution)/shard_map/jvp(...k,kc->...c)/dot_general | solution.py:32
  90.5 3.9 %fusion.110 = (f32[4,10,2048]{2,1,0:T(8,128)S(1)}, f32[4,10,2048]{2,1,0:T(8,128)S(1)}) fusion(f32[2,4,10,2048]{3,2,1,0:T(8,128)} %fusion.10, f32[2,4,10,2048]{3,2,1,0:T(8,128)} %fusion.24, f32[2,4,10,2048]{3,2,1,0:T(8,128)} %fusion.39, f32[2,4,10,2048]{3,2,1,0:T(8,128)S(1)} %fusion.52, f32[4,9,2048]{2,1,0:T(8,128)} %multiply_multiply_fusion.1, ...), kind=kLoop, calls=%fused_computation.103 | loop fusion | flops 1310720 | bytes 4849664 | tf_op jit(solution)/shard_map/jvp()/add | solution.py:73
  96.3 1.8 %fusion.19 = f32[2,4,10,2048]{3,2,1,0:T(8,128)S(1)} fusion(f32[2,4,10,256]{3,2,1,0:T(8,128)} %collective-permute-done.6, s32[256]{0:T(256)S(1)} %bitcast.230), kind=kOutput, calls=%fused_computation.21 | convolution fusion | flops 503840768 | bytes 738304 | tf_op jit(solution)/shard_map/...k,kc->...c/dot_general | solution.py:32
  98.1 1.8 %fusion.34 = f32[2,4,10,2048]{3,2,1,0:T(8,128)S(1)} fusion(f32[2,4,10,256]{3,2,1,0:T(8,128)} %collective-permute-done.5, s32[256]{0:T(256)S(1)} %bitcast.223), kind=kOutput, calls=%fused_computation.30 | convolution fusion | flops 503840768 | bytes 738304 | tf_op jit(solution)/shard_map/...k,kc->...c/dot_general | solution.py:32
  99.9 1.8 %fusion.4 = f32[2,4,10,2048]{3,2,1,0:T(8,128)S(1)} fusion(f32[2,4,10,256]{3,2,1,0:T(8,128)} %collective-permute-done.7, s32[256]{0:T(256)S(1)} %bitcast.237), kind=kOutput, calls=%fused_computation.12 | convolution fusion | flops 503840768 | bytes 738304 | tf_op jit(solution)/shard_map/...k,kc->...c/dot_general | solution.py:32
  101.9 2.1 %fusion.1 = f32[2,4,10,2048]{3,2,1,0:T(8,128)S(1)} fusion(f32[2,4,10,2048]{3,2,1,0:T(8,128)S(1)} %fusion.4, f32[2,4,10,2048]{3,2,1,0:T(8,128)S(1)} %fusion.19, f32[2,4,10,2048]{3,2,1,0:T(8,128)S(1)} %fusion.34, f32[2,4,10,256]{3,2,1,0:T(8,128)} %collective-permute-done.4, s32[256]{0:T(256)S(1)} %bitcast.216), kind=kOutput, calls=%fused_computation.2 | convolution fusion | flops 504332288 | bytes 2704384 | tf_op jit(solution)/shard_map/...k,kc->...c/dot_general | solution.py:32
  106.7 20.9 %all-gather.3.cloned.1.call-done = f32[16,10,2048]{2,1,0:T(8,128)} async-done(((f32[2,10,2048]{2,1,0:T(8,128)}), f32[16,10,2048]{2,1,0:T(8,128)}) %all-gather.3.cloned.1.call-update) | async-done | bytes 1310736 | tf_op jit(solution)/shard_map/all_gather | solution.py:8
  127.6 1.8 %reduce_sum.71 = f32[2,10,2048]{2,1,0:T(8,128)S(1)} reduce(f32[8,2,10,2048]{3,2,1,0:T(8,128)} %bitcast.201, f32[]{:T(128)} %constant.51.clone.1), dimensions={0}, to_apply=%region_6.7 | reduce | flops 286720 | bytes 1474564 | tf_op jit(solution)/shard_map/reduce_sum | solution.py:8
  (95 shorter events, 21.9 us)
Async XLA Ops:
  7.2 120.5 %all-gather.3.cloned.1.call-start = ((), (), s32[]{:S(2)}) async-start(), calls=%async_computation | async-start | bytes 2359296 | tf_op jit(solution)/shard_map/all_gather | solution.py:8
  11.6 25.6 %collective-permute-start.2 = (f32[2,4,10,256]{3,2,1,0:T(8,128)}, f32[2,4,10,256]{3,2,1,0:T(8,128)}, u32[]{:S(2)}, u32[]{:S(2)}) collective-permute-start(f32[2,4,10,256]{3,2,1,0:T(8,128)} %fusion.26), channel_id=1, source_target_pairs={{0,32},{8,40},{16,48},{24,56},{32,0},{40,8},{48,16},{56,24},{64,96... | collective-permute-start | bytes 245768 | tf_op jit(solution)/shard_map/ppermute | solution.py:14
  18.2 14.7 %copy-start.12 = (f32[10,2048]{1,0:T(8,128)S(1)}, f32[10,2048]{1,0:T(8,128)}, u32[]{:S(2)}) copy-start(f32[10,2048]{1,0:T(8,128)} %param.16) | copy-start | bytes 245764
  18.2 14.7 %copy-start.14 = (f32[10,2048]{1,0:T(8,128)S(1)}, f32[10,2048]{1,0:T(8,128)}, u32[]{:S(2)}) copy-start(f32[10,2048]{1,0:T(8,128)} %param.17) | copy-start | bytes 245764
  18.2 14.7 %copy-start.16 = (s32[10,2048]{1,0:T(8,128)S(1)}, s32[10,2048]{1,0:T(8,128)}, u32[]{:S(2)}) copy-start(s32[10,2048]{1,0:T(8,128)} %param.18) | copy-start | bytes 245764
  18.2 22.7 %collective-permute-start.3 = (f32[2,4,10,256]{3,2,1,0:T(8,128)}, f32[2,4,10,256]{3,2,1,0:T(8,128)}, u32[]{:S(2)}, u32[]{:S(2)}) collective-permute-start(f32[2,4,10,256]{3,2,1,0:T(8,128)} %fusion.12), channel_id=1, source_target_pairs={{0,64},{8,72},{16,80},{24,88},{32,96},{40,104},{48,112},{56,120},{... | collective-permute-start | bytes 245768 | tf_op jit(solution)/shard_map/ppermute | solution.py:14
  23.4 9.6 %copy-start.5 = (f32[4,10,2048]{2,0,1:T(4,128)S(1)}, f32[4,10,2048]{2,0,1:T(4,128)}, u32[]{:S(2)}) copy-start(f32[4,10,2048]{2,0,1:T(4,128)} %param.23) | copy-start | bytes 983044
  23.4 9.6 %copy-start.6 = (f32[4,10,2048]{2,0,1:T(4,128)S(1)}, f32[4,10,2048]{2,0,1:T(4,128)}, u32[]{:S(2)}) copy-start(f32[4,10,2048]{2,0,1:T(4,128)} %param.22) | copy-start | bytes 983044
  25.4 18.8 %collective-permute-start.1 = (f32[2,4,10,256]{3,2,1,0:T(8,128)}, f32[2,4,10,256]{3,2,1,0:T(8,128)}, u32[]{:S(2)}, u32[]{:S(2)}) collective-permute-start(f32[2,4,10,256]{3,2,1,0:T(8,128)} %fusion.41), channel_id=1, source_target_pairs={{0,16},{8,24},{16,0},{24,8},{32,48},{40,56},{48,32},{56,40},{64,80... | collective-permute-start | bytes 245768 | tf_op jit(solution)/shard_map/ppermute | solution.py:14
  30.7 17.0 %collective-permute-start = (f32[2,4,10,256]{3,2,1,0:T(8,128)}, f32[2,4,10,256]{3,2,1,0:T(8,128)}, u32[]{:S(2)}, u32[]{:S(2)}) collective-permute-start(f32[2,4,10,256]{3,2,1,0:T(8,128)} %fusion.54), channel_id=1, source_target_pairs={{0,8},{8,0},{16,24},{24,16},{32,40},{40,32},{48,56},{56,48},{64,72... | collective-permute-start | bytes 245768 | tf_op jit(solution)/shard_map/ppermute | solution.py:14
  34.4 2.8 %copy-start.23 = (f32[4,256]{1,0:T(4,128)S(1)}, f32[4,256]{1,0:T(4,128)}, u32[]{:S(2)}) copy-start(f32[4,256]{1,0:T(4,128)} %param.21) | copy-start | bytes 12292
  35.9 5.0 %copy-start.8 = (f32[1,4,10,2048]{3,2,1,0:T(8,128)S(1)}, f32[1,4,10,2048]{3,2,1,0:T(8,128)}, u32[]{:S(2)}) copy-start(f32[1,4,10,2048]{3,2,1,0:T(8,128)} %get-tuple-element.51) | copy-start | bytes 983044
  37.2 3.7 %copy-start.9 = (f32[1,4,10,2048]{3,2,1,0:T(8,128)S(1)}, f32[1,4,10,2048]{3,2,1,0:T(8,128)}, u32[]{:S(2)}) copy-start(f32[1,4,10,2048]{3,2,1,0:T(8,128)} %get-tuple-element.79) | copy-start | bytes 983044
  44.2 6.8 %copy-start.10 = (f32[9,2048]{1,0:T(8,128)S(1)}, f32[9,2048]{1,0:T(8,128)}, u32[]{:S(2)}) copy-start(f32[9,2048]{1,0:T(8,128)} %broadcast_multiply_fusion.4) | copy-start | bytes 221188
  44.2 6.8 %copy-start.11 = (f32[9,2048]{1,0:T(8,128)S(1)}, f32[9,2048]{1,0:T(8,128)}, u32[]{:S(2)}) copy-start(f32[9,2048]{1,0:T(8,128)} %broadcast_multiply_fusion.5) | copy-start | bytes 221188
  44.2 6.8 %copy-start.13 = (f32[10,2048]{1,0:T(8,128)S(1)}, f32[10,2048]{1,0:T(8,128)}, u32[]{:S(2)}) copy-start(f32[10,2048]{1,0:T(8,128)} %param.16) | copy-start | bytes 245764
  44.3 6.8 %copy-start.15 = (f32[10,2048]{1,0:T(8,128)S(1)}, f32[10,2048]{1,0:T(8,128)}, u32[]{:S(2)}) copy-start(f32[10,2048]{1,0:T(8,128)} %param.17) | copy-start | bytes 245764
  44.3 6.8 %copy-start.17 = (s32[10,2048]{1,0:T(8,128)S(1)}, s32[10,2048]{1,0:T(8,128)}, u32[]{:S(2)}) copy-start(s32[10,2048]{1,0:T(8,128)} %param.18) | copy-start | bytes 245764
  44.3 6.8 %copy-start.21 = (f32[10,2048]{1,0:T(8,128)S(1)}, f32[10,2048]{1,0:T(8,128)}, u32[]{:S(2)}) copy-start(f32[10,2048]{1,0:T(8,128)} %param.15) | copy-start | bytes 245764
  52.4 4.8 %copy-start.19 = (f32[2,10,256]{2,1,0:T(8,128)}, f32[2,10,256]{2,1,0:T(8,128)S(1)}, u32[]{:S(2)}) copy-start(f32[2,10,256]{2,1,0:T(8,128)S(1)} %fusion.68) | copy-start | bytes 61444
  56.2 5.3 %copy-start.18 = (f32[2,10,256]{2,1,0:T(8,128)}, f32[2,10,256]{2,1,0:T(8,128)S(1)}, u32[]{:S(2)}) copy-start(f32[2,10,256]{2,1,0:T(8,128)S(1)} %fusion.59) | copy-start | bytes 61444
  63.4 32.9 %collective-permute-start.6 = (f32[2,4,10,256]{3,2,1,0:T(8,128)}, f32[2,4,10,256]{3,2,1,0:T(8,128)}, u32[]{:S(2)}, u32[]{:S(2)}) collective-permute-start(f32[2,4,10,256]{3,2,1,0:T(8,128)} %get-tuple-element.48), channel_id=1, source_target_pairs={{0,32},{8,40},{16,48},{24,56},{32,0},{40,8},{48,16},{56,24},{64,96... | collective-permute-start | bytes 245768 | tf_op jit(solution)/shard_map/ppermute | solution.py:14
  67.4 30.7 %collective-permute-start.5 = (f32[2,4,10,256]{3,2,1,0:T(8,128)}, f32[2,4,10,256]{3,2,1,0:T(8,128)}, u32[]{:S(2)}, u32[]{:S(2)}) collective-permute-start(f32[2,4,10,256]{3,2,1,0:T(8,128)} %get-tuple-element.49), channel_id=1, source_target_pairs={{0,16},{8,24},{16,0},{24,8},{32,48},{40,56},{48,32},{56,40},{64,80... | collective-permute-start | bytes 245768 | tf_op jit(solution)/shard_map/ppermute | solution.py:14
  70.0 29.9 %collective-permute-start.7 = (f32[2,4,10,256]{3,2,1,0:T(8,128)}, f32[2,4,10,256]{3,2,1,0:T(8,128)}, u32[]{:S(2)}, u32[]{:S(2)}) collective-permute-start(f32[2,4,10,256]{3,2,1,0:T(8,128)} %get-tuple-element.47), channel_id=1, source_target_pairs={{0,64},{8,72},{16,80},{24,88},{32,96},{40,104},{48,112},{56,120},{... | collective-permute-start | bytes 245768 | tf_op jit(solution)/shard_map/ppermute | solution.py:14
  76.7 25.1 %collective-permute-start.4 = (f32[2,4,10,256]{3,2,1,0:T(8,128)}, f32[2,4,10,256]{3,2,1,0:T(8,128)}, u32[]{:S(2)}, u32[]{:S(2)}) collective-permute-start(f32[2,4,10,256]{3,2,1,0:T(8,128)} %get-tuple-element.46), channel_id=1, source_target_pairs={{0,8},{8,0},{16,24},{24,16},{32,40},{40,32},{48,56},{56,48},{64,72... | collective-permute-start | bytes 245768 | tf_op jit(solution)/shard_map/ppermute | solution.py:14
  79.4 7.7 %copy-start.20 = (f32[2,10,256]{2,1,0:T(8,128)S(1)}, f32[2,10,256]{2,1,0:T(8,128)}, u32[]{:S(2)}) copy-start(f32[2,10,256]{2,1,0:T(8,128)} %copy-done.19) | copy-start | bytes 61444
  81.4 8.7 %copy-start.22 = (f32[4,2048]{1,0:T(4,128)S(1)}, f32[4,2048]{1,0:T(4,128)}, u32[]{:S(2)}) copy-start(f32[4,2048]{1,0:T(4,128)} %param.19) | copy-start | bytes 98308
  101.8 2.2 %copy-start = (f32[4,9,2048]{2,1,0:T(8,128)S(1)}, f32[4,9,2048]{2,1,0:T(8,128)}, u32[]{:S(2)}) copy-start(f32[4,9,2048]{2,1,0:T(8,128)} %get-tuple-element.35) | copy-start | bytes 884740
  101.8 2.2 %copy-start.1 = (f32[4,9,2048]{2,1,0:T(8,128)S(1)}, f32[4,9,2048]{2,1,0:T(8,128)}, u32[]{:S(2)}) copy-start(f32[4,9,2048]{2,1,0:T(8,128)} %get-tuple-element.36) | copy-start | bytes 884740
  101.8 2.2 %copy-start.2 = (f32[4,9,2048]{2,1,0:T(8,128)S(1)}, f32[4,9,2048]{2,1,0:T(8,128)}, u32[]{:S(2)}) copy-start(f32[4,9,2048]{2,1,0:T(8,128)} %get-tuple-element.59) | copy-start | bytes 884740
  101.8 2.2 %copy-start.3 = (f32[4,9,2048]{2,1,0:T(8,128)S(1)}, f32[4,9,2048]{2,1,0:T(8,128)}, u32[]{:S(2)}) copy-start(f32[4,9,2048]{2,1,0:T(8,128)} %get-tuple-element.33) | copy-start | bytes 884740
  101.8 2.2 %copy-start.4 = (f32[4,9,2048]{2,1,0:T(8,128)S(1)}, f32[4,9,2048]{2,1,0:T(8,128)}, u32[]{:S(2)}) copy-start(f32[4,9,2048]{2,1,0:T(8,128)} %get-tuple-element.34) | copy-start | bytes 884740
  (1 other events, 2.2 us)
Sparse Core Ops, SparseCore 0:
  79.5 48.0 all-gather.2
